TPU v7x, 32 devices: a whole 2x2x4 slice. The times are simulated.
32 devices in a mesh: section: 4 (over y, x), expert: 8 (over z, core).
Axes of the slice: x: 2, y: 2, z: 4, core: 2. Of those that a mesh axis runs over, the one named last changes fastest.
Arguments:
- tokens: bfloat16 [4, 2, 256, 2048], P('section', None, 'expert'), may hold values from -6 to 6
- routes: int32 [4, 2, 256, 2], P('section', None, 'expert'), may hold values from 0 to 3, all different within a row; in each aligned block of 32 rows (0 to 31, 32 to 63, ..., all dimensions but the last counted through in order) at most 24 rows name the same one
- combine_weights: float32 [4, 2, 256, 2], P('section', None, 'expert'), may hold values from 0.3 to 1
- norm_gain: float32 [4, 2048], P('section'), may hold values from 0.5 to 1.5
- gate_up: bfloat16 [4, 8, 2048, 768], P('section', 'expert'), may hold values from -0.125 to 0.125
- down: bfloat16 [4, 8, 384, 2048], P('section', 'expert'), may hold values from -0.21875 to 0.21875
Outputs:
- next_inputs: bfloat16 [4, 2, 256, 2048], P('section', None, 'expert')
Inputs may be any that keep to these rules, and one draw needn't show every extreme that they name: `routes`: each token names 2 different experts. Among the 32 tokens of one device in one section and micro-batch (aligned blocks of 32 rows) no expert is named more than 24 times.
All inputs are finite; a program needn't handle non-finite values.
Results may differ from a plain program's by a relative error of at most 0.0055.
Values may be sent and summed in bfloat16 or wider, within the bound.
No kernel may reach another device: no remote copies, remote signals or barrier semaphores. Data moves between devices by JAX's collectives and lax.ppermute only.
A program may use at most 64 MiB of HBM per device.

v0:
```python
import jax
import jax.numpy as jnp
from jax import lax
from jax.sharding import PartitionSpec as P

EPSILON = 1e-06


def from_behind(value, axis, steps):
    count = lax.axis_size(axis)
    pairs = [(source, (source + steps) % count) for source in range(count)]
    return lax.ppermute(value, axis, pairs)


def slot_codes(route_block, experts, capacity):
    flat = route_block.reshape(-1)
    onehot = (flat[:, None] == jnp.arange(experts, dtype=jnp.int32)[None, :]).astype(jnp.int32)
    before = jnp.cumsum(onehot, axis=0) - onehot
    slot = jnp.sum(before * onehot, axis=1)
    return (flat * capacity + slot).reshape(route_block.shape)


def normalize(block, gain):
    values = block.astype(jnp.float32)
    scale = lax.rsqrt(jnp.mean(values * values, axis=-1, keepdims=True) + EPSILON)
    return (values * scale * gain).astype(jnp.bfloat16)


def expert_half(block, weights_gu, weights_dn):
    shape = block.shape
    token_rows = block.reshape(-1, shape[-1])
    units = weights_dn.shape[0]
    joined = jnp.dot(token_rows, weights_gu, preferred_element_type=jnp.float32)
    hidden = (jax.nn.silu(joined[:, :units]) * joined[:, units:]).astype(jnp.bfloat16)
    partial_out = jnp.dot(hidden, weights_dn, preferred_element_type=jnp.float32).astype(
        jnp.bfloat16
    )
    return partial_out.reshape(shape)


def handoff(layer_out):
    return from_behind(layer_out, "section", 1)


def local(tokens, routes, combine_weights, norm_gain, gate_up, down):
    experts = lax.axis_size("expert") // 2
    tok_count = tokens.shape[2]
    width = tokens.shape[3]
    topk = routes.shape[3]
    capacity = 2 * ((3 * tok_count * topk + 4 * experts - 1) // (4 * experts))
    weights_gu = gate_up[0, 0]
    weights_dn = down[0, 0]
    gain = norm_gain[0]
    inputs = tokens[0]
    choices_in = routes[0]
    weights_in = combine_weights[0]
    pieces = []
    for position in range(inputs.shape[0]):
        section_x = inputs[position : position + 1]
        count = section_x.shape[0]
        normed = normalize(section_x, gain)
        codes = jax.vmap(lambda block: slot_codes(block, experts, capacity))(
            choices_in[position : position + 1]
        )
        lanes = jnp.arange(experts * capacity, dtype=jnp.int32)
        onehot = jnp.any(codes[..., None] == lanes, axis=2).astype(jnp.bfloat16)
        buffer = jnp.einsum("mtq,mtd->qmd", onehot, normed, preferred_element_type=jnp.float32)
        buffer = buffer.astype(jnp.bfloat16).reshape(experts, capacity, count, width)
        outgoing = jnp.repeat(buffer, 2, axis=0)
        incoming = lax.all_to_all(outgoing, "expert", split_axis=0, concat_axis=0, tiled=True)
        parts = expert_half(incoming, weights_gu, weights_dn)
        returned = lax.all_to_all(parts, "expert", split_axis=0, concat_axis=0, tiled=True)
        pairs = returned.reshape(experts, 2, capacity, count, width)
        results = (pairs[:, 0].astype(jnp.float32) + pairs[:, 1].astype(jnp.float32)).astype(
            jnp.bfloat16
        )
        table = jnp.swapaxes(results.reshape(experts * capacity, count, width), 0, 1)
        flat_codes = codes.reshape(count, tok_count * topk)
        picked = table[jnp.arange(count)[:, None], flat_codes].reshape(
            count, tok_count, topk, width
        )
        mixed = section_x.astype(jnp.float32) + jnp.sum(
            weights_in[position : position + 1][..., None] * picked.astype(jnp.float32), axis=2
        )
        finished_layer = mixed.astype(jnp.bfloat16)
        pieces.append(handoff(finished_layer))
    moved = jnp.concatenate(pieces, axis=0)
    return moved[None]


def solution(mesh):
    return jax.shard_map(
        local,
        mesh=mesh,
        in_specs=(
            P("section", None, "expert", None),
            P("section", None, "expert", None),
            P("section", None, "expert", None),
            P("section", None),
            P("section", "expert", None, None),
            P("section", "expert", None, None),
        ),
        out_specs=P("section", None, "expert", None),
        check_vma=False,
    )
```

profile of v0, /device:TPU:0, one launch (start us, length us, event | category | flops | bytes accessed | tf_op | source)
XLA Modules:
  0.0 130.0 jit_solution(14057331167735075358)
XLA Ops:
  4.3 1.3 convolution_convert_fusion.2
  6.6 6.4 %all-to-all-start.2 = ((bf16[8,24,1,2048]{3,1,2,0:T(8,128)(2,1)}), bf16[8,24,1,2048]{3,1,2,0:T(8,128)(2,1)}, u32[]{:S(2)}, u32[]{:S(2)}) async-start(bf16[8,24,1,2048]{3,1,2,0:T(8,128)(2,1)} %bitcast.133), calls=%async_computation.2 | async-start | bytes 1572864 | tf_op jit(solution)/shard_map/all_to_all | solution.py:70
  14.1 20.0 %all-to-all-done.2 = bf16[8,24,1,2048]{3,1,2,0:T(8,128)(2,1)} async-done(((bf16[8,24,1,2048]{3,1,2,0:T(8,128)(2,1)}), bf16[8,24,1,2048]{3,1,2,0:T(8,128)(2,1)}, u32[]{:S(2)}, u32[]{:S(2)}) %all-to-all-start.2) | async-done | bytes 786464 | tf_op jit(solution)/shard_map/all_to_all | solution.py:70
  34.0 2.0 %broadcast_in_dim.10 = bf16[4,2,24,2048]{3,2,1,0:T(8,128)(2,1)} broadcast(bf16[4,24,2048]{2,1,0:T(8,128)(2,1)} %bitcast.135), dimensions={0,2,3} | broadcast | bytes 1179648 | tf_op jit(solution)/shard_map/broadcast_in_dim | solution.py:69
  36.0 4.2 %all-to-all-start = ((bf16[8,24,1,2048]{3,1,2,0:T(8,128)(2,1)}), bf16[8,24,1,2048]{3,1,2,0:T(8,128)(2,1)}, u32[]{:S(2)}, u32[]{:S(2)}) async-start(bf16[8,24,1,2048]{3,1,2,0:T(8,128)(2,1)} %bitcast.134), calls=%async_computation | async-start | bytes 1572864 | tf_op jit(solution)/shard_map/all_to_all | solution.py:70
  40.2 2.0 %fusion = f32[192,768]{1,0:T(8,128)S(1)} fusion(bf16[192,2048]{1,0:T(8,128)(2,1)} %bitcast.28, bf16[1,1,2048,768]{3,2,1,0:T(8,128)(2,1)S(1)} %copy-done), kind=kOutput, calls=%fused_computation.2 | convolution fusion | flops 603979776 | bytes 4521984 | tf_op jit(solution)/shard_map/dot_general | solution.py:33
  42.3 1.5 %convolution_convert_fusion = bf16[192,2048]{1,0:T(8,128)(2,1)} fusion(bf16[1,1,384,2048]{3,2,1,0:T(8,128)(2,1)S(1)} %copy-done.6, f32[192,768]{1,0:T(8,128)S(1)} %fusion), kind=kOutput, calls=%fused_computation.6 | convolution fusion | flops 302825472 | bytes 2949120 | tf_op jit(solution)/shard_map/dot_general | solution.py:35
  43.8 17.4 %all-to-all-done = bf16[8,24,1,2048]{3,1,2,0:T(8,128)(2,1)} async-done(((bf16[8,24,1,2048]{3,1,2,0:T(8,128)(2,1)}), bf16[8,24,1,2048]{3,1,2,0:T(8,128)(2,1)}, u32[]{:S(2)}, u32[]{:S(2)}) %all-to-all-start) | async-done | bytes 786464 | tf_op jit(solution)/shard_map/all_to_all | solution.py:70
  61.2 4.2 %all-to-all-start.3 = ((bf16[8,24,1,2048]{3,1,2,0:T(8,128)(2,1)}), bf16[8,24,1,2048]{3,1,2,0:T(8,128)(2,1)}, u32[]{:S(2)}, u32[]{:S(2)}) async-start(bf16[8,24,1,2048]{3,1,2,0:T(8,128)(2,1)} %bitcast.138), calls=%async_computation.3 | async-start | bytes 1572864 | tf_op jit(solution)/shard_map/all_to_all | solution.py:72
  65.6 2.0 %fusion.2 = f32[192,768]{1,0:T(8,128)S(1)} fusion(bf16[192,2048]{1,0:T(8,128)(2,1)} %bitcast.9, bf16[1,1,2048,768]{3,2,1,0:T(8,128)(2,1)S(1)} %copy-done), kind=kOutput, calls=%fused_computation.4 | convolution fusion | flops 603979776 | bytes 4521984 | tf_op jit(solution)/shard_map/dot_general | solution.py:33
  67.6 1.5 %convolution_convert_fusion.1 = bf16[192,2048]{1,0:T(8,128)(2,1)} fusion(bf16[1,1,384,2048]{3,2,1,0:T(8,128)(2,1)S(1)} %copy-done.7, f32[192,768]{1,0:T(8,128)S(1)} %fusion.2), kind=kOutput, calls=%fused_computation.7 | convolution fusion | flops 302825472 | bytes 2949120 | tf_op jit(solution)/shard_map/dot_general | solution.py:35
  69.1 17.2 %all-to-all-done.3 = bf16[8,24,1,2048]{3,1,2,0:T(8,128)(2,1)} async-done(((bf16[8,24,1,2048]{3,1,2,0:T(8,128)(2,1)}), bf16[8,24,1,2048]{3,1,2,0:T(8,128)(2,1)}, u32[]{:S(2)}, u32[]{:S(2)}) %all-to-all-start.3) | async-done | bytes 786464 | tf_op jit(solution)/shard_map/all_to_all | solution.py:72
  86.3 4.2 %all-to-all-start.1 = ((bf16[8,24,1,2048]{3,1,2,0:T(8,128)(2,1)}), bf16[8,24,1,2048]{3,1,2,0:T(8,128)(2,1)}, u32[]{:S(2)}, u32[]{:S(2)}) async-start(bf16[8,24,1,2048]{3,1,2,0:T(8,128)(2,1)} %bitcast.137), calls=%async_computation.1 | async-start | bytes 1572864 | tf_op jit(solution)/shard_map/all_to_all | solution.py:72
  93.4 2.1 %gather_fusion.1 = bf16[64,2048]{1,0:T(8,128)(2,1)} fusion(bf16[1,96,2048]{2,1,0:T(8,128)(2,1)S(1)} %bitcast.131, s32[64]{0:T(128)S(1)} %or_bitcast_fusion), kind=kCustom, calls=%fused_computation.1 | custom fusion | bytes 524800 | tf_op jit(solution)/shard_map/gather | solution.py:79
  95.5 2.1 %reshape.660 = f32[1,32,2,2048]{3,2,1,0:T(2,128)} reshape(bf16[64,2048]{1,0:T(8,128)(2,1)} %gather_fusion.1) | data formatting | bytes 786432 | tf_op jit(solution)/shard_map/convert_element_type | solution.py:83
  97.6 13.9 %all-to-all-done.1 = bf16[8,24,1,2048]{3,1,2,0:T(8,128)(2,1)} async-done(((bf16[8,24,1,2048]{3,1,2,0:T(8,128)(2,1)}), bf16[8,24,1,2048]{3,1,2,0:T(8,128)(2,1)}, u32[]{:S(2)}, u32[]{:S(2)}) %all-to-all-start.1) | async-done | bytes 786464 | tf_op jit(solution)/shard_map/all_to_all | solution.py:72
  112.7 2.1 %gather_fusion = bf16[64,2048]{1,0:T(8,128)(2,1)} fusion(bf16[1,96,2048]{2,1,0:T(8,128)(2,1)S(1)} %bitcast.132, s32[64]{0:T(128)S(1)} %or_bitcast_fusion.1), kind=kCustom, calls=%fused_computation | custom fusion | bytes 524800 | tf_op jit(solution)/shard_map/gather | solution.py:79
  114.8 2.1 %reshape.657 = f32[1,32,2,2048]{3,2,1,0:T(2,128)} reshape(bf16[64,2048]{1,0:T(8,128)(2,1)} %gather_fusion) | data formatting | bytes 786432 | tf_op jit(solution)/shard_map/convert_element_type | solution.py:83
  116.9 1.8 %multiply_reduce_fusion = f32[32,2048]{1,0:T(8,128)S(1)} fusion(f32[1,32,2,2048]{3,2,1,0:T(2,128)} %reshape.660, f32[32,2]{1,0:T(8,128)} %copy.58), kind=kLoop, calls=%fused_computation.14 | loop fusion | flops 196608 | bytes 786688 | tf_op jit(solution)/shard_map/reduce_sum | solution.py:82
  118.7 1.8 %multiply_reduce_fusion.1 = f32[32,2048]{1,0:T(8,128)S(1)} fusion(f32[1,32,2,2048]{3,2,1,0:T(2,128)} %reshape.657, f32[32,2]{1,0:T(8,128)S(1)} %copy-done.3), kind=kLoop, calls=%fused_computation.15 | loop fusion | flops 196608 | bytes 786688 | tf_op jit(solution)/shard_map/reduce_sum | solution.py:82
  120.6 1.5 %collective-permute-start = (bf16[1,32,2048]{2,1,0:T(8,128)(2,1)S(1)}, bf16[1,32,2048]{2,1,0:T(8,128)(2,1)S(1)}, u32[]{:S(2)}, u32[]{:S(2)}) collective-permute-start(bf16[1,32,2048]{2,1,0:T(8,128)(2,1)S(1)} %get-tuple-element.7), channel_id=1, source_target_pairs={{0,8},{8,16},{16,24},{24,0},{1,9},{9,17},{17,25},{25,1},{2,10},{10... | collective-permute-start | bytes 393224 | tf_op jit(solution)/shard_map/ppermute | solution.py:12
  122.1 1.5 %collective-permute-start.1 = (bf16[1,32,2048]{2,1,0:T(8,128)(2,1)S(1)}, bf16[1,32,2048]{2,1,0:T(8,128)(2,1)S(1)}, u32[]{:S(2)}, u32[]{:S(2)}) collective-permute-start(bf16[1,32,2048]{2,1,0:T(8,128)(2,1)S(1)} %get-tuple-element.8), channel_id=1, source_target_pairs={{0,8},{8,16},{16,24},{24,0},{1,9},{9,17},{17,25},{25,1},{2,10},{10... | collective-permute-start | bytes 393224 | tf_op jit(solution)/shard_map/ppermute | solution.py:12
  123.6 4.3 %collective-permute-done = bf16[1,32,2048]{2,1,0:T(8,128)(2,1)S(1)} collective-permute-done((bf16[1,32,2048]{2,1,0:T(8,128)(2,1)S(1)}, bf16[1,32,2048]{2,1,0:T(8,128)(2,1)S(1)}, u32[]{:S(2)}, u32[]{:S(2)}) %collective-permute-start) | collective-permute-done | bytes 131104 | tf_op jit(solution)/shard_map/ppermute | solution.py:12
  127.9 1.4 %collective-permute-done.1 = bf16[1,32,2048]{2,1,0:T(8,128)(2,1)S(1)} collective-permute-done((bf16[1,32,2048]{2,1,0:T(8,128)(2,1)S(1)}, bf16[1,32,2048]{2,1,0:T(8,128)(2,1)S(1)}, u32[]{:S(2)}, u32[]{:S(2)}) %collective-permute-start.1) | collective-permute-done | bytes 131104 | tf_op jit(solution)/shard_map/ppermute | solution.py:12
  (54 shorter events, 11.4 us)
Async XLA Ops:
  0.0 40.2 %copy-start = (bf16[1,1,2048,768]{3,2,1,0:T(8,128)(2,1)S(1)}, bf16[1,1,2048,768]{3,2,1,0:T(8,128)(2,1)}, u32[]{:S(2)}) copy-start(bf16[1,1,2048,768]{3,2,1,0:T(8,128)(2,1)} %param.10) | copy-start | bytes 9437188
  4.3 8.7 %copy-start.1 = (bf16[1,2,32,2048]{3,2,1,0:T(8,128)(2,1)S(1)}, bf16[1,2,32,2048]{3,2,1,0:T(8,128)(2,1)}, u32[]{:S(2)}) copy-start(bf16[1,2,32,2048]{3,2,1,0:T(8,128)(2,1)} %param.6) | copy-start | bytes 786436
  4.3 8.7 %copy-start.4 = (f32[1,2048]{1,0:T(1,128)S(1)}, f32[1,2048]{1,0:T(1,128)}, u32[]{:S(2)}) copy-start(f32[1,2048]{1,0:T(1,128)} %param.9) | copy-start | bytes 24580
  6.6 27.4 %all-to-all-start.2 = ((bf16[8,24,1,2048]{3,1,2,0:T(8,128)(2,1)}), bf16[8,24,1,2048]{3,1,2,0:T(8,128)(2,1)}, u32[]{:S(2)}, u32[]{:S(2)}) async-start(bf16[8,24,1,2048]{3,1,2,0:T(8,128)(2,1)} %bitcast.133), calls=%async_computation.2 | async-start | bytes 1572864 | tf_op jit(solution)/shard_map/all_to_all | solution.py:70
  36.0 25.2 %all-to-all-start = ((bf16[8,24,1,2048]{3,1,2,0:T(8,128)(2,1)}), bf16[8,24,1,2048]{3,1,2,0:T(8,128)(2,1)}, u32[]{:S(2)}, u32[]{:S(2)}) async-start(bf16[8,24,1,2048]{3,1,2,0:T(8,128)(2,1)} %bitcast.134), calls=%async_computation | async-start | bytes 1572864 | tf_op jit(solution)/shard_map/all_to_all | solution.py:70
  40.2 2.1 %copy-start.6 = (bf16[1,1,384,2048]{3,2,1,0:T(8,128)(2,1)S(1)}, bf16[1,1,384,2048]{3,2,1,0:T(8,128)(2,1)}, u32[]{:S(2)}) copy-start(bf16[1,1,384,2048]{3,2,1,0:T(8,128)(2,1)} %param.11) | copy-start | bytes 4718596
  43.8 21.8 %copy-start.5 = (f32[1,2,32,2]{2,3,1,0:T(2,128)S(1)}, f32[1,2,32,2]{2,3,1,0:T(2,128)}, u32[]{:S(2)}) copy-start(f32[1,2,32,2]{2,3,1,0:T(2,128)} %param.8) | copy-start | bytes 1540
  61.2 25.2 %all-to-all-start.3 = ((bf16[8,24,1,2048]{3,1,2,0:T(8,128)(2,1)}), bf16[8,24,1,2048]{3,1,2,0:T(8,128)(2,1)}, u32[]{:S(2)}, u32[]{:S(2)}) async-start(bf16[8,24,1,2048]{3,1,2,0:T(8,128)(2,1)} %bitcast.138), calls=%async_computation.3 | async-start | bytes 1572864 | tf_op jit(solution)/shard_map/all_to_all | solution.py:72
  65.6 2.0 %copy-start.7 = (bf16[1,1,384,2048]{3,2,1,0:T(8,128)(2,1)S(1)}, bf16[1,1,384,2048]{3,2,1,0:T(8,128)(2,1)}, u32[]{:S(2)}) copy-start(bf16[1,1,384,2048]{3,2,1,0:T(8,128)(2,1)} %param.11) | copy-start | bytes 4718596
  86.3 25.2 %all-to-all-start.1 = ((bf16[8,24,1,2048]{3,1,2,0:T(8,128)(2,1)}), bf16[8,24,1,2048]{3,1,2,0:T(8,128)(2,1)}, u32[]{:S(2)}, u32[]{:S(2)}) async-start(bf16[8,24,1,2048]{3,1,2,0:T(8,128)(2,1)} %bitcast.137), calls=%async_computation.1 | async-start | bytes 1572864 | tf_op jit(solution)/shard_map/all_to_all | solution.py:72
  114.8 3.9 %copy-start.3 = (f32[32,2]{1,0:T(8,128)S(1)}, f32[32,2]{1,0:T(8,128)}, u32[]{:S(2)}) copy-start(f32[32,2]{1,0:T(8,128)} %copy.51) | copy-start | bytes 772
  114.8 5.7 %copy-start.2 = (bf16[1,2,32,2048]{3,2,1,0:T(8,128)(2,1)S(1)}, bf16[1,2,32,2048]{3,2,1,0:T(8,128)(2,1)}, u32[]{:S(2)}) copy-start(bf16[1,2,32,2048]{3,2,1,0:T(8,128)(2,1)} %param.6) | copy-start | bytes 786436
  120.6 7.3 %collective-permute-start = (bf16[1,32,2048]{2,1,0:T(8,128)(2,1)S(1)}, bf16[1,32,2048]{2,1,0:T(8,128)(2,1)S(1)}, u32[]{:S(2)}, u32[]{:S(2)}) collective-permute-start(bf16[1,32,2048]{2,1,0:T(8,128)(2,1)S(1)} %get-tuple-element.7), channel_id=1, source_target_pairs={{0,8},{8,16},{16,24},{24,0},{1,9},{9,17},{17,25},{25,1},{2,10},{10... | collective-permute-start | bytes 393224 | tf_op jit(solution)/shard_map/ppermute | solution.py:12
  122.1 7.2 %collective-permute-start.1 = (bf16[1,32,2048]{2,1,0:T(8,128)(2,1)S(1)}, bf16[1,32,2048]{2,1,0:T(8,128)(2,1)S(1)}, u32[]{:S(2)}, u32[]{:S(2)}) collective-permute-start(bf16[1,32,2048]{2,1,0:T(8,128)(2,1)S(1)} %get-tuple-element.8), channel_id=1, source_target_pairs={{0,8},{8,16},{16,24},{24,0},{1,9},{9,17},{17,25},{25,1},{2,10},{10... | collective-permute-start | bytes 393224 | tf_op jit(solution)/shard_map/ppermute | solution.py:12
where the time goes:
time: 131 us; the launch traced here: 130 us
  waiting for transfers between devices  74.1 us (57%)
  starting transfers between devices  22 us (17%)
  local copies, waits for them, and re-layouts  14 us (11%)
  other arithmetic  10.3 us (8%)
  matrix products  9.4 us (7%)
    all_to_all x2, waiting for transfers between devices, local(): lax.all_to_all(outgoing, 'expert', split_axis=0, concat_axis=0, tiled=True)  37.3 us
    all_to_all x2, waiting for transfers between devices, local(): lax.all_to_all(parts, 'expert', split_axis=0, concat_axis=0, tiled=True)  31.1 us
    all_to_all x2, starting transfers between devices, local(): lax.all_to_all(outgoing, 'expert', split_axis=0, concat_axis=0, tiled=True)  10.6 us
    all_to_all x2, starting transfers between devices, local(): lax.all_to_all(parts, 'expert', split_axis=0, concat_axis=0, tiled=True)  8.4 us
    ppermute x2, waiting for transfers between devices, from_behind(): return lax.ppermute(value, axis, pairs)  5.67 us
    gather x2, local copies, waits for them, and re-layouts, local(): table[jnp.arange(count)[:, None], flat_codes]  4.22 us
    convert_element_type x2, local copies, waits for them, and re-layouts, local(): picked.astype(jnp.float32)  4.21 us
    dot_general x2, matrix products, expert_half(): joined = jnp.dot(token_rows, weights_gu, preferred_element_type=jnp.float32)  4.06 us
  transfers between devices with their start and end apart: 6, of which 6 were waited for; matrix products, arithmetic and copies ran while one was open for 12% of the time, Pallas kernels for 0%

commit v1 on v0

--- a/solution.py
+++ b/solution.py
@@ -4,6 +4,22 @@
 from jax.sharding import PartitionSpec as P
 
 EPSILON = 1e-06
+
+
+def swapped_with_each(value, axis, split, join):
+    ways, here = (lax.axis_size(axis), lax.axis_index(axis))
+    width = value.shape[split] // ways
+    shape = list(value.shape)
+    shape[split] = width
+    height = shape[join]
+    shape[join] = height * ways
+    full = jnp.zeros(shape, value.dtype)
+    for mask in range(ways):
+        part = lax.dynamic_slice_in_dim(value, (here ^ mask) * width, width, axis=split)
+        if mask:
+            part = lax.ppermute(part, axis, [(d, d ^ mask) for d in range(ways)])
+        full = lax.dynamic_update_slice_in_dim(full, part, (here ^ mask) * height, axis=join)
+    return full
 
 
 def from_behind(value, axis, steps):
@@ -69,7 +85,7 @@
         outgoing = jnp.repeat(buffer, 2, axis=0)
         incoming = lax.all_to_all(outgoing, "expert", split_axis=0, concat_axis=0, tiled=True)
         parts = expert_half(incoming, weights_gu, weights_dn)
-        returned = lax.all_to_all(parts, "expert", split_axis=0, concat_axis=0, tiled=True)
+        returned = swapped_with_each(parts, "expert", 0, 0)
         pairs = returned.reshape(experts, 2, capacity, count, width)
         results = (pairs[:, 0].astype(jnp.float32) + pairs[:, 1].astype(jnp.float32)).astype(
             jnp.bfloat16

time: 131 us -> 122 us (0.931)
  waiting for transfers between devices: 74.1 us -> 41.8 us
  local copies, waits for them, and re-layouts: 14 us -> 31.8 us
  starting transfers between devices: 22 us -> 29.9 us
  matrix products: 9.4 us -> 7.62 us
    all_to_all x2 -> x0, waiting for transfers between devices: 31.1 us -> none  [local(): lax.all_to_all(parts, 'expert', split_axis=0, concat_axis=0, tiled=True)]
    ppermute x0 -> x14, starting transfers between devices: none -> 16.3 us  [swapped_with_each(): part = lax.ppermute(part, axis, [(d, d ^ mask) for d in range(ways)])]
    dynamic_update_slice x0 -> x14, local copies, waits for them, and re-layouts: none -> 14.3 us  [swapped_with_each(): lax.dynamic_update_slice_in_dim(full, part, (here ^ mask) * height, axis=...]
    all_to_all x2 -> x0, starting transfers between devices: 8.4 us -> none  [local(): lax.all_to_all(parts, 'expert', split_axis=0, concat_axis=0, tiled=True)]
    all_to_all x2, waiting for transfers between devices: 37.3 us -> 30.5 us  [local(): lax.all_to_all(outgoing, 'expert', split_axis=0, concat_axis=0, tiled=True)]
    ppermute x0 -> x14, waiting for transfers between devices: none -> 5.03 us  [swapped_with_each(): part = lax.ppermute(part, axis, [(d, d ^ mask) for d in range(ways)])]
    another operation x0 -> x2, local copies, waits for them, and re-layouts: none -> 1.94 us
    dot_general x2, matrix products: 2.99 us -> 1.19 us  [expert_half(): jnp.dot(hidden, weights_dn, preferred_element_type=jnp.float32)]
  transfers between devices with their start and end apart: 6 -> 18, of which waited for: 6 -> 5; matrix products, arithmetic and copies ran while one was open for 12% -> 24% of each run, Pallas kernels for 0% -> 0%
where the time goes in v1:
time: 122 us
  waiting for transfers between devices  41.8 us (34%)
  local copies, waits for them, and re-layouts  31.8 us (26%)
  starting transfers between devices  29.9 us (25%)
  other arithmetic  10.3 us (8%)
  matrix products  7.62 us (6%)
    all_to_all x2, waiting for transfers between devices, local(): lax.all_to_all(outgoing, 'expert', split_axis=0, concat_axis=0, tiled=True)  30.5 us
    ppermute x14, starting transfers between devices, swapped_with_each(): part = lax.ppermute(part, axis, [(d, d ^ mask) for d in range(ways)])  16.3 us
    dynamic_update_slice x14, local copies, waits for them, and re-layouts, swapped_with_each(): lax.dynamic_update_slice_in_dim(full, part, (here ^ mask) * height, axis=...  14.3 us
    all_to_all x2, starting transfers between devices, local(): lax.all_to_all(outgoing, 'expert', split_axis=0, concat_axis=0, tiled=True)  10.6 us
    ppermute x2, waiting for transfers between devices, from_behind(): return lax.ppermute(value, axis, pairs)  6.25 us
    ppermute x14, waiting for transfers between devices, swapped_with_each(): part = lax.ppermute(part, axis, [(d, d ^ mask) for d in range(ways)])  5.03 us
    convert_element_type x2, local copies, waits for them, and re-layouts, local(): picked.astype(jnp.float32)  4.23 us
    gather x2, local copies, waits for them, and re-layouts, local(): table[jnp.arange(count)[:, None], flat_codes]  4.22 us
  transfers between devices with their start and end apart: 18, of which 5 were waited for; matrix products, arithmetic and copies ran while one was open for 24% of the time, Pallas kernels for 0%

profile of v1, /device:TPU:0, one launch (start us, length us, event | category | flops | bytes accessed | tf_op | source)
XLA Modules:
  0.0 121.7 jit_solution(5265029174641017672)
XLA Ops:
  6.6 6.4 %all-to-all-start.1 = ((bf16[8,24,1,2048]{3,1,2,0:T(8,128)(2,1)}), bf16[8,24,1,2048]{3,1,2,0:T(8,128)(2,1)}, u32[]{:S(2)}, u32[]{:S(2)}) async-start(bf16[8,24,1,2048]{3,1,2,0:T(8,128)(2,1)} %bitcast.114), calls=%async_computation.1 | async-start | bytes 1572864 | tf_op jit(solution)/shard_map/all_to_all | solution.py:86
  14.5 19.5 %all-to-all-done.1 = bf16[8,24,1,2048]{3,1,2,0:T(8,128)(2,1)} async-done(((bf16[8,24,1,2048]{3,1,2,0:T(8,128)(2,1)}), bf16[8,24,1,2048]{3,1,2,0:T(8,128)(2,1)}, u32[]{:S(2)}, u32[]{:S(2)}) %all-to-all-start.1) | async-done | bytes 786464 | tf_op jit(solution)/shard_map/all_to_all | solution.py:86
  34.0 2.0 %broadcast_in_dim.10 = bf16[4,2,24,2048]{3,2,1,0:T(8,128)(2,1)} broadcast(bf16[4,24,2048]{2,1,0:T(8,128)(2,1)} %bitcast.115), dimensions={0,2,3} | broadcast | bytes 1179648 | tf_op jit(solution)/shard_map/broadcast_in_dim | solution.py:85
  36.0 4.2 %all-to-all-start = ((bf16[8,24,1,2048]{3,1,2,0:T(8,128)(2,1)}), bf16[8,24,1,2048]{3,1,2,0:T(8,128)(2,1)}, u32[]{:S(2)}, u32[]{:S(2)}) async-start(bf16[8,24,1,2048]{3,1,2,0:T(8,128)(2,1)} %bitcast.113), calls=%async_computation | async-start | bytes 1572864 | tf_op jit(solution)/shard_map/all_to_all | solution.py:86
  41.7 2.0 %fusion = f32[192,768]{1,0:T(8,128)S(1)} fusion(bf16[192,2048]{1,0:T(8,128)(2,1)} %bitcast.27, bf16[1,1,2048,768]{3,2,1,0:T(8,128)(2,1)S(1)} %copy-done), kind=kOutput, calls=%fused_computation.2 | convolution fusion | flops 603979776 | bytes 4521984 | tf_op jit(solution)/shard_map/dot_general | solution.py:49
  46.4 1.6 %collective-permute-start.9 = (bf16[1,24,1,2048]{3,1,0,2:T(8,128)(2,1)}, bf16[1,24,1,2048]{3,1,0,2:T(8,128)(2,1)}, u32[]{:S(2)}, u32[]{:S(2)}) collective-permute-start(bf16[1,24,1,2048]{3,1,0,2:T(8,128)(2,1)} %get-tuple-element.20), channel_id=1, source_target_pairs={{0,2},{1,3},{2,0},{3,1},{4,6},{5,7},{6,4},{7,5},{8,10},{9,11},{10,... | collective-permute-start | bytes 294920 | tf_op jit(solution)/shard_map/ppermute | solution.py:20
  48.1 2.7 %collective-permute-start.11 = (bf16[1,24,1,2048]{3,1,0,2:T(8,128)(2,1)S(1)}, bf16[1,24,1,2048]{3,1,0,2:T(8,128)(2,1)}, u32[]{:S(2)}, u32[]{:S(2)}) collective-permute-start(bf16[1,24,1,2048]{3,1,0,2:T(8,128)(2,1)S(1)} %get-tuple-element.18), channel_id=1, source_target_pairs={{0,4},{1,5},{2,6},{3,7},{4,0},{5,1},{6,2},{7,3},{8,12},{9,13},{10,... | collective-permute-start | bytes 294920 | tf_op jit(solution)/shard_map/ppermute | solution.py:20
  50.8 11.0 %all-to-all-done = bf16[8,24,1,2048]{3,1,2,0:T(8,128)(2,1)} async-done(((bf16[8,24,1,2048]{3,1,2,0:T(8,128)(2,1)}), bf16[8,24,1,2048]{3,1,2,0:T(8,128)(2,1)}, u32[]{:S(2)}, u32[]{:S(2)}) %all-to-all-start) | async-done | bytes 786464 | tf_op jit(solution)/shard_map/all_to_all | solution.py:86
  61.9 2.0 %fusion.2 = f32[192,768]{1,0:T(8,128)S(1)} fusion(bf16[192,2048]{1,0:T(8,128)(2,1)} %bitcast.9, bf16[1,1,2048,768]{3,2,1,0:T(8,128)(2,1)S(1)} %copy-done), kind=kOutput, calls=%fused_computation.4 | convolution fusion | flops 603979776 | bytes 4521984 | tf_op jit(solution)/shard_map/dot_general | solution.py:49
  71.3 1.9 %collective-permute-start = (bf16[1,24,1,2048]{3,1,0,2:T(8,128)(2,1)S(1)}, bf16[1,24,1,2048]{3,1,0,2:T(8,128)(2,1)S(1)}, u32[]{:S(2)}, u32[]{:S(2)}) collective-permute-start(bf16[1,24,1,2048]{3,1,0,2:T(8,128)(2,1)S(1)} %get-tuple-element.13), channel_id=1, source_target_pairs={{0,1},{1,0},{2,3},{3,2},{4,5},{5,4},{6,7},{7,6},{8,9},{9,8},{10,11... | collective-permute-start | bytes 294920 | tf_op jit(solution)/shard_map/ppermute | solution.py:20
  74.8 1.5 %constant_dynamic-update-slice_fusion.2 = bf16[8,24,1,2048]{3,1,0,2:T(8,128)(2,1)} fusion(bf16[8,24,1,2048]{3,1,0,2:T(8,128)(2,1)} %constant_dynamic-update-slice_fusion.3, bf16[1,24,1,2048]{3,1,0,2:T(8,128)(2,1)} %collective-permute-done.11, s32[]{:T(128)S(6)} %select_n.76), kind=kLoop, calls=%fused_computation.64 | loop fusion | bytes 196612 | tf_op jit(solution)/shard_map/dynamic_update_slice | solution.py:21
  80.0 2.9 %collective-permute-start.4 = (bf16[1,24,1,2048]{3,1,0,2:T(8,128)(2,1)S(1)}, bf16[1,24,1,2048]{3,1,0,2:T(8,128)(2,1)S(1)}, u32[]{:S(2)}, u32[]{:S(2)}) collective-permute-start(bf16[1,24,1,2048]{3,1,0,2:T(8,128)(2,1)S(1)} %get-tuple-element.9), channel_id=1, source_target_pairs={{0,5},{1,4},{2,7},{3,6},{4,1},{5,0},{6,3},{7,2},{8,13},{9,12},{10,... | collective-permute-start | bytes 294920 | tf_op jit(solution)/shard_map/ppermute | solution.py:20
  86.4 2.2 %collective-permute-start.6 = (bf16[1,24,1,2048]{3,1,0,2:T(8,128)(2,1)}, bf16[1,24,1,2048]{3,1,0,2:T(8,128)(2,1)}, u32[]{:S(2)}, u32[]{:S(2)}) collective-permute-start(bf16[1,24,1,2048]{3,1,0,2:T(8,128)(2,1)} %get-tuple-element.7), channel_id=1, source_target_pairs={{0,7},{1,6},{2,5},{3,4},{4,3},{5,2},{6,1},{7,0},{8,15},{9,14},{10,... | collective-permute-start | bytes 294920 | tf_op jit(solution)/shard_map/ppermute | solution.py:20
  90.5 5.0 %collective-permute-done.4 = bf16[1,24,1,2048]{3,1,0,2:T(8,128)(2,1)S(1)} collective-permute-done((bf16[1,24,1,2048]{3,1,0,2:T(8,128)(2,1)S(1)}, bf16[1,24,1,2048]{3,1,0,2:T(8,128)(2,1)S(1)}, u32[]{:S(2)}, u32[]{:S(2)}) %collective-permute-start.4) | collective-permute-done | bytes 98336 | tf_op jit(solution)/shard_map/ppermute | solution.py:20
  96.8 2.1 %gather_fusion.1 = bf16[64,2048]{1,0:T(8,128)(2,1)} fusion(bf16[1,96,2048]{2,1,0:T(8,128)(2,1)S(1)} %bitcast.111, s32[64]{0:T(128)S(1)} %or_bitcast_fusion), kind=kCustom, calls=%fused_computation.1 | custom fusion | bytes 524800 | tf_op jit(solution)/shard_map/gather | solution.py:95
  98.9 2.1 %reshape.660 = f32[1,32,2,2048]{3,2,1,0:T(2,128)} reshape(bf16[64,2048]{1,0:T(8,128)(2,1)} %gather_fusion.1) | data formatting | bytes 786432 | tf_op jit(solution)/shard_map/convert_element_type | solution.py:99
  101.0 1.5 %constant_dynamic-update-slice_fusion.6 = bf16[8,24,1,2048]{3,1,0,2:T(8,128)(2,1)} fusion(bf16[8,24,1,2048]{3,1,0,2:T(8,128)(2,1)} %constant_dynamic-update-slice_fusion.7, bf16[1,24,1,2048]{3,1,0,2:T(8,128)(2,1)} %collective-permute-done.6, s32[]{:T(128)S(6)} %select_n.79), kind=kLoop, calls=%fused_computation.72 | loop fusion | bytes 196612 | tf_op jit(solution)/shard_map/dynamic_update_slice | solution.py:21
  103.8 2.1 %gather_fusion = bf16[64,2048]{1,0:T(8,128)(2,1)} fusion(bf16[1,96,2048]{2,1,0:T(8,128)(2,1)S(1)} %bitcast.112, s32[64]{0:T(128)S(1)} %or_bitcast_fusion.1), kind=kCustom, calls=%fused_computation | custom fusion | bytes 524800 | tf_op jit(solution)/shard_map/gather | solution.py:95
  105.9 2.1 %reshape.657 = f32[1,32,2,2048]{3,2,1,0:T(2,128)} reshape(bf16[64,2048]{1,0:T(8,128)(2,1)} %gather_fusion) | data formatting | bytes 786432 | tf_op jit(solution)/shard_map/convert_element_type | solution.py:99
  108.0 1.8 %multiply_reduce_fusion = f32[32,2048]{1,0:T(8,128)S(1)} fusion(f32[1,32,2,2048]{3,2,1,0:T(2,128)} %reshape.660, f32[32,2]{1,0:T(8,128)} %copy.41), kind=kLoop, calls=%fused_computation.14 | loop fusion | flops 196608 | bytes 786688 | tf_op jit(solution)/shard_map/reduce_sum | solution.py:98
  109.8 1.8 %multiply_reduce_fusion.1 = f32[32,2048]{1,0:T(8,128)S(1)} fusion(f32[1,32,2,2048]{3,2,1,0:T(2,128)} %reshape.657, f32[32,2]{1,0:T(8,128)S(1)} %copy-done.3), kind=kLoop, calls=%fused_computation.15 | loop fusion | flops 196608 | bytes 786688 | tf_op jit(solution)/shard_map/reduce_sum | solution.py:98
  111.7 1.5 %collective-permute-start.15 = (bf16[1,32,2048]{2,1,0:T(8,128)(2,1)S(1)}, bf16[1,32,2048]{2,1,0:T(8,128)(2,1)S(1)}, u32[]{:S(2)}, u32[]{:S(2)}) collective-permute-start(bf16[1,32,2048]{2,1,0:T(8,128)(2,1)S(1)} %get-tuple-element.24), channel_id=1, source_target_pairs={{0,8},{8,16},{16,24},{24,0},{1,9},{9,17},{17,25},{25,1},{2,10},{10... | collective-permute-start | bytes 393224 | tf_op jit(solution)/shard_map/ppermute | solution.py:28
  114.7 4.3 %collective-permute-done.15 = bf16[1,32,2048]{2,1,0:T(8,128)(2,1)S(1)} collective-permute-done((bf16[1,32,2048]{2,1,0:T(8,128)(2,1)S(1)}, bf16[1,32,2048]{2,1,0:T(8,128)(2,1)S(1)}, u32[]{:S(2)}, u32[]{:S(2)}) %collective-permute-start.15) | collective-permute-done | bytes 131104 | tf_op jit(solution)/shard_map/ppermute | solution.py:28
  119.0 2.0 %collective-permute-done.7 = bf16[1,32,2048]{2,1,0:T(8,128)(2,1)S(1)} collective-permute-done((bf16[1,32,2048]{2,1,0:T(8,128)(2,1)S(1)}, bf16[1,32,2048]{2,1,0:T(8,128)(2,1)S(1)}, u32[]{:S(2)}, u32[]{:S(2)}) %collective-permute-start.7) | collective-permute-done | bytes 131104 | tf_op jit(solution)/shard_map/ppermute | solution.py:28
  (95 shorter events, 34.9 us)
Async XLA Ops:
  0.0 41.6 %copy-start = (bf16[1,1,2048,768]{3,2,1,0:T(8,128)(2,1)S(1)}, bf16[1,1,2048,768]{3,2,1,0:T(8,128)(2,1)}, u32[]{:S(2)}) copy-start(bf16[1,1,2048,768]{3,2,1,0:T(8,128)(2,1)} %param.10) | copy-start | bytes 9437188
  4.3 9.1 %copy-start.5 = (f32[1,2,32,2]{2,3,1,0:T(2,128)S(1)}, f32[1,2,32,2]{2,3,1,0:T(2,128)}, u32[]{:S(2)}) copy-start(f32[1,2,32,2]{2,3,1,0:T(2,128)} %param.8) | copy-start | bytes 1540
  4.3 9.1 %copy-start.1 = (bf16[1,2,32,2048]{3,2,1,0:T(8,128)(2,1)S(1)}, bf16[1,2,32,2048]{3,2,1,0:T(8,128)(2,1)}, u32[]{:S(2)}) copy-start(bf16[1,2,32,2048]{3,2,1,0:T(8,128)(2,1)} %param.6) | copy-start | bytes 786436
  4.3 9.1 %copy-start.4 = (f32[1,2048]{1,0:T(1,128)S(1)}, f32[1,2048]{1,0:T(1,128)}, u32[]{:S(2)}) copy-start(f32[1,2048]{1,0:T(1,128)} %param.9) | copy-start | bytes 24580
  6.6 27.4 %all-to-all-start.1 = ((bf16[8,24,1,2048]{3,1,2,0:T(8,128)(2,1)}), bf16[8,24,1,2048]{3,1,2,0:T(8,128)(2,1)}, u32[]{:S(2)}, u32[]{:S(2)}) async-start(bf16[8,24,1,2048]{3,1,2,0:T(8,128)(2,1)} %bitcast.114), calls=%async_computation.1 | async-start | bytes 1572864 | tf_op jit(solution)/shard_map/all_to_all | solution.py:86
  36.0 25.9 %all-to-all-start = ((bf16[8,24,1,2048]{3,1,2,0:T(8,128)(2,1)}), bf16[8,24,1,2048]{3,1,2,0:T(8,128)(2,1)}, u32[]{:S(2)}, u32[]{:S(2)}) async-start(bf16[8,24,1,2048]{3,1,2,0:T(8,128)(2,1)} %bitcast.113), calls=%async_computation | async-start | bytes 1572864 | tf_op jit(solution)/shard_map/all_to_all | solution.py:86
  46.1 20.1 %collective-permute-start.8 = (bf16[1,24,1,2048]{3,1,0,2:T(8,128)(2,1)}, bf16[1,24,1,2048]{3,1,0,2:T(8,128)(2,1)}, u32[]{:S(2)}, u32[]{:S(2)}) collective-permute-start(bf16[1,24,1,2048]{3,1,0,2:T(8,128)(2,1)} %get-tuple-element.21), channel_id=1, source_target_pairs={{0,1},{1,0},{2,3},{3,2},{4,5},{5,4},{6,7},{7,6},{8,9},{9,8},{10,11... | collective-permute-start | bytes 294920 | tf_op jit(solution)/shard_map/ppermute | solution.py:20
  46.4 22.2 %collective-permute-start.9 = (bf16[1,24,1,2048]{3,1,0,2:T(8,128)(2,1)}, bf16[1,24,1,2048]{3,1,0,2:T(8,128)(2,1)}, u32[]{:S(2)}, u32[]{:S(2)}) collective-permute-start(bf16[1,24,1,2048]{3,1,0,2:T(8,128)(2,1)} %get-tuple-element.20), channel_id=1, source_target_pairs={{0,2},{1,3},{2,0},{3,1},{4,6},{5,7},{6,4},{7,5},{8,10},{9,11},{10,... | collective-permute-start | bytes 294920 | tf_op jit(solution)/shard_map/ppermute | solution.py:20
  48.1 23.2 %collective-permute-start.10 = (bf16[1,24,1,2048]{3,1,0,2:T(8,128)(2,1)}, bf16[1,24,1,2048]{3,1,0,2:T(8,128)(2,1)}, u32[]{:S(2)}, u32[]{:S(2)}) collective-permute-start(bf16[1,24,1,2048]{3,1,0,2:T(8,128)(2,1)} %get-tuple-element.19), channel_id=1, source_target_pairs={{0,3},{1,2},{2,1},{3,0},{4,7},{5,6},{6,5},{7,4},{8,11},{9,10},{10,... | collective-permute-start | bytes 294920 | tf_op jit(solution)/shard_map/ppermute | solution.py:20
  48.1 26.7 %collective-permute-start.11 = (bf16[1,24,1,2048]{3,1,0,2:T(8,128)(2,1)S(1)}, bf16[1,24,1,2048]{3,1,0,2:T(8,128)(2,1)}, u32[]{:S(2)}, u32[]{:S(2)}) collective-permute-start(bf16[1,24,1,2048]{3,1,0,2:T(8,128)(2,1)S(1)} %get-tuple-element.18), channel_id=1, source_target_pairs={{0,4},{1,5},{2,6},{3,7},{4,0},{5,1},{6,2},{7,3},{8,12},{9,13},{10,... | collective-permute-start | bytes 294920 | tf_op jit(solution)/shard_map/ppermute | solution.py:20
  50.7 25.6 %collective-permute-start.12 = (bf16[1,24,1,2048]{3,1,0,2:T(8,128)(2,1)S(1)}, bf16[1,24,1,2048]{3,1,0,2:T(8,128)(2,1)}, u32[]{:S(2)}, u32[]{:S(2)}) collective-permute-start(bf16[1,24,1,2048]{3,1,0,2:T(8,128)(2,1)S(1)} %get-tuple-element.17), channel_id=1, source_target_pairs={{0,5},{1,4},{2,7},{3,6},{4,1},{5,0},{6,3},{7,2},{8,13},{9,12},{10,... | collective-permute-start | bytes 294920 | tf_op jit(solution)/shard_map/ppermute | solution.py:20
  66.2 13.0 %collective-permute-start.13 = (bf16[1,24,1,2048]{3,1,0,2:T(8,128)(2,1)S(1)}, bf16[1,24,1,2048]{3,1,0,2:T(8,128)(2,1)S(1)}, u32[]{:S(2)}, u32[]{:S(2)}) collective-permute-start(bf16[1,24,1,2048]{3,1,0,2:T(8,128)(2,1)S(1)} %get-tuple-element.16), channel_id=1, source_target_pairs={{0,6},{1,7},{2,4},{3,5},{4,2},{5,3},{6,0},{7,1},{8,14},{9,15},{10,... | collective-permute-start | bytes 294920 | tf_op jit(solution)/shard_map/ppermute | solution.py:20
  68.7 11.3 %collective-permute-start.14 = (bf16[1,24,1,2048]{3,1,0,2:T(8,128)(2,1)S(1)}, bf16[1,24,1,2048]{3,1,0,2:T(8,128)(2,1)S(1)}, u32[]{:S(2)}, u32[]{:S(2)}) collective-permute-start(bf16[1,24,1,2048]{3,1,0,2:T(8,128)(2,1)S(1)} %get-tuple-element.15), channel_id=1, source_target_pairs={{0,7},{1,6},{2,5},{3,4},{4,3},{5,2},{6,1},{7,0},{8,15},{9,14},{10,... | collective-permute-start | bytes 294920 | tf_op jit(solution)/shard_map/ppermute | solution.py:20
  71.3 13.5 %collective-permute-start = (bf16[1,24,1,2048]{3,1,0,2:T(8,128)(2,1)S(1)}, bf16[1,24,1,2048]{3,1,0,2:T(8,128)(2,1)S(1)}, u32[]{:S(2)}, u32[]{:S(2)}) collective-permute-start(bf16[1,24,1,2048]{3,1,0,2:T(8,128)(2,1)S(1)} %get-tuple-element.13), channel_id=1, source_target_pairs={{0,1},{1,0},{2,3},{3,2},{4,5},{5,4},{6,7},{7,6},{8,9},{9,8},{10,11... | collective-permute-start | bytes 294920 | tf_op jit(solution)/shard_map/ppermute | solution.py:20
  74.8 11.6 %collective-permute-start.1 = (bf16[1,24,1,2048]{3,1,0,2:T(8,128)(2,1)S(1)}, bf16[1,24,1,2048]{3,1,0,2:T(8,128)(2,1)S(1)}, u32[]{:S(2)}, u32[]{:S(2)}) collective-permute-start(bf16[1,24,1,2048]{3,1,0,2:T(8,128)(2,1)S(1)} %get-tuple-element.12), channel_id=1, source_target_pairs={{0,2},{1,3},{2,0},{3,1},{4,6},{5,7},{6,4},{7,5},{8,10},{9,11},{10,... | collective-permute-start | bytes 294920 | tf_op jit(solution)/shard_map/ppermute | solution.py:20
  76.3 12.9 %collective-permute-start.2 = (bf16[1,24,1,2048]{3,1,0,2:T(8,128)(2,1)S(1)}, bf16[1,24,1,2048]{3,1,0,2:T(8,128)(2,1)S(1)}, u32[]{:S(2)}, u32[]{:S(2)}) collective-permute-start(bf16[1,24,1,2048]{3,1,0,2:T(8,128)(2,1)S(1)} %get-tuple-element.11), channel_id=1, source_target_pairs={{0,3},{1,2},{2,1},{3,0},{4,7},{5,6},{6,5},{7,4},{8,11},{9,10},{10,... | collective-permute-start | bytes 294920 | tf_op jit(solution)/shard_map/ppermute | solution.py:20
  79.2 10.7 %collective-permute-start.3 = (bf16[1,24,1,2048]{3,1,0,2:T(8,128)(2,1)S(1)}, bf16[1,24,1,2048]{3,1,0,2:T(8,128)(2,1)S(1)}, u32[]{:S(2)}, u32[]{:S(2)}) collective-permute-start(bf16[1,24,1,2048]{3,1,0,2:T(8,128)(2,1)S(1)} %get-tuple-element.10), channel_id=1, source_target_pairs={{0,4},{1,5},{2,6},{3,7},{4,0},{5,1},{6,2},{7,3},{8,12},{9,13},{10,... | collective-permute-start | bytes 294920 | tf_op jit(solution)/shard_map/ppermute | solution.py:20
  80.0 15.6 %collective-permute-start.4 = (bf16[1,24,1,2048]{3,1,0,2:T(8,128)(2,1)S(1)}, bf16[1,24,1,2048]{3,1,0,2:T(8,128)(2,1)S(1)}, u32[]{:S(2)}, u32[]{:S(2)}) collective-permute-start(bf16[1,24,1,2048]{3,1,0,2:T(8,128)(2,1)S(1)} %get-tuple-element.9), channel_id=1, source_target_pairs={{0,5},{1,4},{2,7},{3,6},{4,1},{5,0},{6,3},{7,2},{8,13},{9,12},{10,... | collective-permute-start | bytes 294920 | tf_op jit(solution)/shard_map/ppermute | solution.py:20
  84.8 11.4 %collective-permute-start.5 = (bf16[1,24,1,2048]{3,1,0,2:T(8,128)(2,1)S(1)}, bf16[1,24,1,2048]{3,1,0,2:T(8,128)(2,1)S(1)}, u32[]{:S(2)}, u32[]{:S(2)}) collective-permute-start(bf16[1,24,1,2048]{3,1,0,2:T(8,128)(2,1)S(1)} %get-tuple-element.8), channel_id=1, source_target_pairs={{0,6},{1,7},{2,4},{3,5},{4,2},{5,3},{6,0},{7,1},{8,14},{9,15},{10,... | collective-permute-start | bytes 294920 | tf_op jit(solution)/shard_map/ppermute | solution.py:20
  86.4 14.7 %collective-permute-start.6 = (bf16[1,24,1,2048]{3,1,0,2:T(8,128)(2,1)}, bf16[1,24,1,2048]{3,1,0,2:T(8,128)(2,1)}, u32[]{:S(2)}, u32[]{:S(2)}) collective-permute-start(bf16[1,24,1,2048]{3,1,0,2:T(8,128)(2,1)} %get-tuple-element.7), channel_id=1, source_target_pairs={{0,7},{1,6},{2,5},{3,4},{4,3},{5,2},{6,1},{7,0},{8,15},{9,14},{10,... | collective-permute-start | bytes 294920 | tf_op jit(solution)/shard_map/ppermute | solution.py:20
  105.9 3.9 %copy-start.3 = (f32[32,2]{1,0:T(8,128)S(1)}, f32[32,2]{1,0:T(8,128)}, u32[]{:S(2)}) copy-start(f32[32,2]{1,0:T(8,128)} %copy.37) | copy-start | bytes 772
  105.9 5.7 %copy-start.2 = (bf16[1,2,32,2048]{3,2,1,0:T(8,128)(2,1)S(1)}, bf16[1,2,32,2048]{3,2,1,0:T(8,128)(2,1)}, u32[]{:S(2)}) copy-start(bf16[1,2,32,2048]{3,2,1,0:T(8,128)(2,1)} %param.6) | copy-start | bytes 786436
  111.7 7.3 %collective-permute-start.15 = (bf16[1,32,2048]{2,1,0:T(8,128)(2,1)S(1)}, bf16[1,32,2048]{2,1,0:T(8,128)(2,1)S(1)}, u32[]{:S(2)}, u32[]{:S(2)}) collective-permute-start(bf16[1,32,2048]{2,1,0:T(8,128)(2,1)S(1)} %get-tuple-element.24), channel_id=1, source_target_pairs={{0,8},{8,16},{16,24},{24,0},{1,9},{9,17},{17,25},{25,1},{2,10},{10... | collective-permute-start | bytes 393224 | tf_op jit(solution)/shard_map/ppermute | solution.py:28
  113.2 7.7 %collective-permute-start.7 = (bf16[1,32,2048]{2,1,0:T(8,128)(2,1)S(1)}, bf16[1,32,2048]{2,1,0:T(8,128)(2,1)S(1)}, u32[]{:S(2)}, u32[]{:S(2)}) collective-permute-start(bf16[1,32,2048]{2,1,0:T(8,128)(2,1)S(1)} %get-tuple-element.23), channel_id=1, source_target_pairs={{0,8},{8,16},{16,24},{24,0},{1,9},{9,17},{17,25},{25,1},{2,10},{10... | collective-permute-start | bytes 393224 | tf_op jit(solution)/shard_map/ppermute | solution.py:28
  (2 other events, 4.1 us)
